TPU v7x, 256 devices: a whole 4x4x8 slice. The times are simulated.
256 devices in a mesh: seq: 64 (over z, y, core), tensor: 4 (over x).
Axes of the slice: x: 4, y: 4, z: 8, core: 2. Of those that a mesh axis runs over, the one named last changes fastest.
Arguments:
- new_states: bfloat16 [4, 128, 1024], P(None, None, 'tensor'), may hold values from -6 to 6
- self_query: bfloat16 [1024, 1024], P(None, 'tensor'), may hold values from -0.1875 to 0.1875
- self_key: bfloat16 [1024, 1024], P(None, 'tensor'), may hold values from -0.375 to 0.375
- self_value: bfloat16 [1024, 1024], P(None, 'tensor'), may hold values from -0.1875 to 0.1875
- self_output: bfloat16 [1024, 1024], P('tensor'), may hold values from -0.1875 to 0.1875
- cross_query: bfloat16 [1024, 1024], P(None, 'tensor'), may hold values from -0.1875 to 0.1875
- cross_output: bfloat16 [1024, 1024], P('tensor'), may hold values from -0.1875 to 0.1875
- feed_up: bfloat16 [1024, 4096], P(None, 'tensor'), may hold values from -0.1875 to 0.1875
- feed_down: bfloat16 [4096, 1024], P('tensor'), may hold values from -0.09375 to 0.09375
- norm_self: float32 [1024], replicated, may hold values from 0.25 to 1.75
- norm_cross: float32 [1024], replicated, may hold values from 0.25 to 1.75
- norm_feed: float32 [1024], replicated, may hold values from 0.25 to 1.75
- self_cache: bfloat16 [1536, 2, 128, 1024], P('seq', None, None, 'tensor'), may hold values from -240 to 240
- cross_cache: bfloat16 [128, 2, 512, 1024], P(None, None, 'seq', 'tensor'), may hold values from -240 to 240
- cache_lengths: int32 [128], replicated, may hold values from 1 to 16384, as said below
- page_table: int32 [128, 128], replicated, may hold values from -1 to 1535, as said below
- request_order: int32 [128], replicated, may hold values from 0 to 127, each once
- encoder_lengths: int32 [128], replicated, may hold values from 1 to 512, as said below
Outputs:
- out: bfloat16 [4, 128, 1024], P(None, None, 'tensor')
Inputs may be any that keep to these rules, and one draw needn't show every extreme that they name: `cache_lengths`: one request has exactly 16384 cached tokens. `page_table`: row r holds the slots of request r's pages in order: its first ceil(cache_lengths[r] / 128) entries are slots, page p holding positions p * 128 to (p + 1) * 128 - 1, and no slot appears twice in the table; the other entries are -1. Slot s belongs to seq index s // 24. `encoder_lengths`: one request has exactly 512 encoder positions.
All inputs are finite; a program needn't handle non-finite values.
Results may differ from a plain program's by a relative error of at most 0.014.
The roundings to bfloat16 on the way count: a program that leaves them out, or rounds other values in their place, can miss the bound.
Values may be sent and summed in bfloat16 or wider, within the bound.
No kernel may reach another device: no remote copies, remote signals or barrier semaphores. Data moves between devices by JAX's collectives and lax.ppermute only.
A program may use at most 64 MiB of HBM per device.

v0:
```python
import jax
import jax.numpy as jnp
from jax import lax
from jax.sharding import PartitionSpec as P

HEAD_DIM = 64
EPSILON = 1e-05
NEG_FILL = -1e30


def layer_norm(summed, gain):
    center = jnp.mean(summed, axis=-1, keepdims=True)
    spread = jnp.mean(summed * summed, axis=-1, keepdims=True) - center * center
    return (summed - center) * lax.rsqrt(spread + EPSILON) * gain


def global_max(local_max):
    return lax.pmax(local_max, "seq")


def global_totals(denom, numer):
    return lax.psum((denom, numer), "seq")


def reduce_norm(residual, partial_value, gain):
    width = residual.shape[1]
    total = lax.psum(partial_value, "tensor")
    full = layer_norm(residual.astype(jnp.float32) + total, gain).astype(jnp.bfloat16)
    columns = width // lax.axis_size("tensor")
    return (full, lax.dynamic_slice_in_dim(full, lax.axis_index("tensor") * columns, columns, 1))


def on_device(
    new_states,
    self_query,
    self_key,
    self_value,
    self_output,
    cross_query,
    cross_output,
    feed_up,
    feed_down,
    norm_self,
    norm_cross,
    norm_feed,
    self_cache,
    cross_cache,
    cache_lengths,
    page_table,
    request_order,
    encoder_lengths,
):
    states = lax.all_gather(new_states, "tensor", axis=2, tiled=True)
    steps, requests, width = states.shape
    flat = states.reshape(steps * requests, width)
    local_width = self_query.shape[1]
    local_heads = local_width // HEAD_DIM
    scaling = HEAD_DIM ** (-0.5)
    queries = (jnp.dot(flat, self_query, preferred_element_type=jnp.float32) * scaling).astype(
        jnp.bfloat16
    )
    new_keys = jnp.dot(flat, self_key, preferred_element_type=jnp.float32).astype(jnp.bfloat16)
    new_values = jnp.dot(flat, self_value, preferred_element_type=jnp.float32).astype(jnp.bfloat16)
    query_grid = queries.reshape(steps, requests, local_heads, HEAD_DIM)
    key_grid = new_keys.reshape(steps, requests, local_heads, HEAD_DIM)
    value_grid = new_values.reshape(steps, requests, local_heads, HEAD_DIM)
    slot_count = self_cache.shape[0]
    page_width = self_cache.shape[2]
    max_pages = page_table.shape[1]
    seq_index = lax.axis_index("seq")
    flat_table = page_table.reshape(-1)
    entry_ids = jnp.arange(requests * max_pages, dtype=jnp.int32)
    entry_request = entry_ids // max_pages
    entry_page = entry_ids % max_pages
    slot_ids = seq_index * slot_count + jnp.arange(slot_count, dtype=jnp.int32)
    matches = flat_table[None, :] == slot_ids[:, None]
    slot_live = jnp.any(matches, axis=1)
    slot_owner = jnp.sum(jnp.where(matches, entry_request[None, :], 0), axis=1)
    slot_page = jnp.sum(jnp.where(matches, entry_page[None, :], 0), axis=1)
    request_ids = jnp.arange(requests, dtype=jnp.int32)
    slot_length = jnp.sum(
        jnp.where(slot_owner[:, None] == request_ids[None, :], cache_lengths[None, :], 0), axis=1
    )
    positions = slot_page[:, None] * page_width + jnp.arange(page_width, dtype=jnp.int32)[None, :]
    slot_valid = slot_live[:, None] & (positions < slot_length[:, None])
    slot_rows = slot_live[:, None] & (request_order[None, :] == slot_owner[:, None])
    rows_half = slot_rows.astype(jnp.bfloat16)
    rows_wide = slot_rows.astype(jnp.float32)
    slot_query = jnp.einsum(
        "pb,sbc->psc",
        rows_half,
        queries.reshape(steps, requests, local_width),
        preferred_element_type=jnp.float32,
    ).astype(jnp.bfloat16)
    slot_query = slot_query.reshape(slot_count, steps, local_heads, HEAD_DIM)
    cache_keys = self_cache[:, 0].reshape(slot_count, page_width, local_heads, HEAD_DIM)
    cache_values = self_cache[:, 1].reshape(slot_count, page_width, local_heads, HEAD_DIM)
    cache_scores = jnp.einsum(
        "pshd,pkhd->pshk", slot_query, cache_keys, preferred_element_type=jnp.float32
    )
    valid_grid = slot_valid[:, None, None, :]
    slot_max = jnp.max(jnp.where(valid_grid, cache_scores, NEG_FILL), axis=3)
    row_max = jnp.max(
        jnp.where(slot_rows[:, None, :, None], slot_max[:, :, None, :], NEG_FILL), axis=0
    )
    causal = jnp.arange(steps)[None, :] <= jnp.arange(steps)[:, None]
    new_scores = jnp.einsum(
        "tbhd,ubhd->bhtu", query_grid, key_grid, preferred_element_type=jnp.float32
    )
    new_scores = jnp.where(causal, new_scores, NEG_FILL)
    new_max = jnp.transpose(jnp.max(new_scores, axis=3), (2, 0, 1))
    top = global_max(jnp.maximum(row_max, new_max))
    slot_top = jnp.einsum("pb,sbh->psh", rows_wide, top, precision=lax.Precision.HIGHEST)
    cache_weights = jnp.exp(jnp.where(valid_grid, cache_scores - slot_top[..., None], NEG_FILL))
    cache_denom = jnp.sum(cache_weights, axis=3)
    cache_numer = jnp.einsum(
        "pshk,pkhd->pshd",
        cache_weights.astype(jnp.bfloat16),
        cache_values,
        preferred_element_type=jnp.float32,
    )
    row_denom = jnp.einsum("pb,psh->sbh", rows_wide, cache_denom, precision=lax.Precision.HIGHEST)
    row_numer = jnp.einsum("pb,pshd->sbhd", rows_wide, cache_numer, precision=lax.Precision.HIGHEST)
    total_denom, total_numer = global_totals(row_denom, row_numer)
    top_new = jnp.transpose(top, (1, 2, 0))[..., None]
    new_weights = jnp.where(causal, jnp.exp(new_scores - top_new), 0.0)
    new_denom = jnp.transpose(jnp.sum(new_weights, axis=3), (2, 0, 1))
    new_numer = jnp.einsum(
        "bhtu,ubhd->tbhd",
        new_weights.astype(jnp.bfloat16),
        value_grid,
        preferred_element_type=jnp.float32,
    )
    self_attn = ((total_numer + new_numer) / (total_denom + new_denom)[..., None]).astype(
        jnp.bfloat16
    )
    partial_value = jnp.dot(
        self_attn.reshape(steps * requests, local_width),
        self_output,
        preferred_element_type=jnp.float32,
    )
    first_full, first_share = reduce_norm(flat, partial_value, norm_self)
    cross_queries = (
        jnp.dot(first_full, cross_query, preferred_element_type=jnp.float32) * scaling
    ).astype(jnp.bfloat16)
    cross_grid = cross_queries.reshape(steps, requests, local_heads, HEAD_DIM)
    order_rows = (request_order[:, None] == request_ids[None, :]).astype(jnp.bfloat16)
    request_query = jnp.einsum(
        "br,sbhd->srhd", order_rows, cross_grid, preferred_element_type=jnp.float32
    ).astype(jnp.bfloat16)
    enc_local = cross_cache.shape[2]
    enc_keys = cross_cache[:, 0].reshape(requests, enc_local, local_heads, HEAD_DIM)
    enc_values = cross_cache[:, 1].reshape(requests, enc_local, local_heads, HEAD_DIM)
    enc_positions = seq_index * enc_local + jnp.arange(enc_local, dtype=jnp.int32)
    enc_valid = (enc_positions[None, :] < encoder_lengths[:, None])[None, :, None, :]
    enc_scores = jnp.einsum(
        "srhd,rehd->srhe", request_query, enc_keys, preferred_element_type=jnp.float32
    )
    enc_top = global_max(jnp.max(jnp.where(enc_valid, enc_scores, NEG_FILL), axis=3))
    enc_weights = jnp.exp(jnp.where(enc_valid, enc_scores - enc_top[..., None], NEG_FILL))
    enc_numer_local = jnp.einsum(
        "srhe,rehd->srhd",
        enc_weights.astype(jnp.bfloat16),
        enc_values,
        preferred_element_type=jnp.float32,
    )
    enc_denom, enc_numer = global_totals(jnp.sum(enc_weights, axis=3), enc_numer_local)
    enc_attn = (enc_numer / enc_denom[..., None]).astype(jnp.bfloat16)
    cross_attn = jnp.einsum(
        "br,srhd->sbhd", order_rows, enc_attn, preferred_element_type=jnp.float32
    ).astype(jnp.bfloat16)
    partial_value = jnp.dot(
        cross_attn.reshape(steps * requests, local_width),
        cross_output,
        preferred_element_type=jnp.float32,
    )
    second_full, second_share = reduce_norm(first_full, partial_value, norm_cross)
    ffn_hidden = jax.nn.gelu(
        jnp.dot(second_full, feed_up, preferred_element_type=jnp.float32), approximate=False
    ).astype(jnp.bfloat16)
    ignored, out_share = reduce_norm(
        second_full, jnp.dot(ffn_hidden, feed_down, preferred_element_type=jnp.float32), norm_feed
    )
    return out_share.reshape(steps, requests, out_share.shape[1])


def solution(mesh):
    in_specs = (
        P(None, None, "tensor"),
        P(None, "tensor"),
        P(None, "tensor"),
        P(None, "tensor"),
        P("tensor", None),
        P(None, "tensor"),
        P("tensor", None),
        P(None, "tensor"),
        P("tensor", None),
        P(),
        P(),
        P(),
        P("seq", None, None, "tensor"),
        P(None, None, "seq", "tensor"),
        P(),
        P(),
        P(),
        P(),
    )
    out_specs = P(None, None, "tensor")
    return jax.shard_map(
        on_device, mesh=mesh, in_specs=in_specs, out_specs=out_specs, check_vma=False
    )
```

profile of v0, /device:TPU:1, one launch (start us, length us, event | category | flops | bytes accessed | tf_op | source)
XLA Modules:
  0.0 1101.1 jit_solution(13234853274242562757)
XLA Ops:
  6.5 0.7 all-gather.2.cloned.1.call-update
  7.3 3.9 fusion.134
  11.2 2.6 copy.103
  13.8 2.7 copy.147
  16.5 0.6 fusion.10
  17.3 0.4 compare_reduce_fusion
  17.8 21.5 %all-gather.2.cloned.1.call-done = bf16[4,128,1024]{2,1,0:T(8,128)(2,1)} async-done(((bf16[4,128,256]{2,1,0:T(8,128)(2,1)}), bf16[4,128,1024]{2,1,0:T(8,128)(2,1)}) %all-gather.2.cloned.1.call-update) | async-done | bytes 1048592 | tf_op jit(solution)/shard_map/all_gather | solution.py:53
  39.3 1.7 fusion.12
  41.0 1.0 reshape.249
  42.0 0.2 convolution_convert_fusion.4
  42.3 2.0 select_reduce_fusion.2
  44.4 2.2 convolution_convert_fusion.3
  46.6 2.0 reshape.250
  48.7 3.0 fusion.62
  51.7 1.6 copy.110
  53.6 128.2 %pmax.14 = f32[4,128,4]{1,2,0:T(4,128)S(1)} all-reduce(f32[4,128,4]{1,2,0:T(4,128)S(1)} %fusion.99), channel_id=1, replica_groups=mesh['seq'=64,'tensor'=4] {'seq'}, use_global_device_ids=true, to_apply=%region_7.8 | all-reduce | flops 2048 | bytes 16384 | tf_op jit(solution)/shard_map/pmax | solution.py:18
  181.8 0.2 fusion.132
  182.1 0.4 fusion.75
  182.7 2.4 convolution_bitcast_fusion.2
  185.1 1.5 convolution_bitcast_fusion.1
  186.6 1.2 copy.119
  187.9 1.5 convolution_convert_fusion.2
  189.3 1.1 reshape.251
  190.4 1.9 fusion.60
  192.3 0.2 convolution_bitcast_fusion.4
  192.5 1.2 copy.120
  193.8 129.3 %psum.50 = f32[4,128,4]{1,2,0:T(4,128)S(1)} all-reduce(f32[4,128,4]{1,2,0:T(4,128)S(1)} %convolution_bitcast_fusion.4), channel_id=1, replica_groups=mesh['seq'=64,'tensor'=4] {'seq'}, use_global_device_ids=true, to_apply=%region_10.11 | all-reduce | flops 2048 | bytes 16384 | tf_op jit(solution)/shard_map/psum | solution.py:22
  323.1 44.2 %all-reduce.6.cloned.1.call-done = f32[4,128,4,64]{1,3,2,0:T(8,128)} async-done(((f32[4,128,4,64]{1,3,2,0:T(8,128)}), f32[4,128,4,64]{1,3,2,0:T(8,128)}) %all-reduce.6.cloned.1.call-update) | async-done | bytes 524304 | tf_op jit(solution)/shard_map/psum | solution.py:22
  367.3 1.3 fusion.59
  368.6 0.2 copy.124
  368.8 1.8 fusion.71
  370.7 0.2 all-reduce.10.cloned.1.call-start
  370.9 2.1 fusion.135
  373.0 1.2 copy.148
  374.2 3.5 copy.129
  377.7 2.2 copy.149
  379.9 3.4 copy.131
  383.4 50.2 %all-reduce.8.cloned.1.call-done = f32[512,1024]{1,0:T(8,128)} async-done(((f32[512,1024]{1,0:T(8,128)}), f32[512,1024]{1,0:T(8,128)}) %all-reduce.8.cloned.1.call-update) | async-done | bytes 2097168 | tf_op jit(solution)/shard_map/psum | solution.py:27
  433.6 2.2 fusion.48
  435.8 0.3 copy-done.5
  436.1 0.5 multiply_convert_fusion.1
  436.6 0.6 copy-done.15
  437.1 0.4 fusion.13
  437.6 1.0 reshape.252
  438.6 1.4 fusion.14
  440.0 1.2 copy.128
  441.2 4.0 select_reduce_fusion
  445.1 246.6 %pmax.15 = f32[4,128,4]{0,2,1:T(4,128)S(1)} all-reduce(f32[4,128,4]{0,2,1:T(4,128)} %get-tuple-element.30), channel_id=1, replica_groups=mesh['seq'=64,'tensor'=4] {'seq'}, use_global_device_ids=true, to_apply=%region_16.17 | all-reduce | flops 2048 | bytes 16384 | tf_op jit(solution)/shard_map/pmax | solution.py:18
  691.8 3.4 fusion.52
  695.2 2.4 copy.132
  697.7 3.1 fusion.50
  700.8 246.8 %psum.53 = f32[4,128,4]{0,2,1:T(4,128)S(1)} all-reduce(f32[4,128,4]{0,2,1:T(4,128)} %fusion.50), channel_id=1, replica_groups=mesh['seq'=64,'tensor'=4] {'seq'}, use_global_device_ids=true, to_apply=%region_19.20 | all-reduce | flops 2048 | bytes 16384 | tf_op jit(solution)/shard_map/psum | solution.py:22
  947.7 1.4 fusion.15
  949.1 0.2 copy.134
  949.3 1.8 fusion.68
  951.1 0.3 all-reduce.14.cloned.1.call-start
  951.4 63.0 %all-reduce.12.cloned.1.call-done = f32[512,1024]{1,0:T(8,128)} async-done(((f32[512,1024]{1,0:T(8,128)}), f32[512,1024]{1,0:T(8,128)}) %all-reduce.12.cloned.1.call-update) | async-done | bytes 2097168 | tf_op jit(solution)/shard_map/psum | solution.py:27
  1014.4 2.2 fusion.49
  1016.6 1.4 multiply_convert_fusion
  1018.1 9.5 fusion.16
  1027.6 0.8 dynamic-slice
  1028.5 62.9 %all-reduce.14.cloned.1.call-done = f32[512,1024]{1,0:T(8,128)} async-done(((f32[512,1024]{1,0:T(8,128)}), f32[512,1024]{1,0:T(8,128)}) %all-reduce.14.cloned.1.call-update) | async-done | bytes 2097168 | tf_op jit(solution)/shard_map/psum | solution.py:27
  1091.4 2.0 fusion.133
  1093.4 0.9 fusion.56
  (64 shorter events, 1.6 us)
Async XLA Ops:
  6.5 1011.5 %copy-start = (bf16[1024,1024]{1,0:T(8,128)(2,1)S(1)}, bf16[1024,1024]{1,0:T(8,128)(2,1)}, u32[]{:S(2)}) copy-start(bf16[1024,1024]{1,0:T(8,128)(2,1)} %param.26) | copy-start | bytes 6291460
  6.5 32.7 %all-gather.2.cloned.1.call-start = ((), (), s32[]{:S(2)}) async-start(), calls=%async_computation | async-start | bytes 1310720 | tf_op jit(solution)/shard_map/all_gather | solution.py:53
  7.3 360.1 %all-reduce.6.cloned.1.call-start = ((), (), s32[]{:S(2)}) async-start(), calls=%async_computation.1 | async-start | bytes 1048576 | tf_op jit(solution)/shard_map/psum | solution.py:22
  13.8 2.7 copy-start.9
  13.8 3.3 copy-start.16
  13.8 3.9 copy-start.10
  13.8 25.4 %copy-start.14 = (bf16[1024,256]{1,0:T(8,128)(2,1)S(1)}, bf16[1024,256]{1,0:T(8,128)(2,1)}, u32[]{:S(2)}) copy-start(bf16[1024,256]{1,0:T(8,128)(2,1)} %param.19) | copy-start | bytes 1572868
  40.9 3.5 copy-start.3
  186.6 247.0 %all-reduce.8.cloned.1.call-start = ((), (), s32[]{:S(2)}) async-start(), calls=%async_computation.2 | async-start | bytes 4194304 | tf_op jit(solution)/shard_map/psum | solution.py:27
  193.7 175.1 %copy-start.7 = (bf16[256,1024]{1,0:T(8,128)(2,1)S(1)}, bf16[256,1024]{1,0:T(8,128)(2,1)}, u32[]{:S(2)}) copy-start(bf16[256,1024]{1,0:T(8,128)(2,1)} %param.22) | copy-start | bytes 1572868
  370.7 577.0 %all-reduce.10.cloned.1.call-start = ((), (), s32[]{:S(2)}) async-start(), calls=%async_computation.3 | async-start | bytes 1048576 | tf_op jit(solution)/shard_map/psum | solution.py:22
  374.2 9.1 copy-start.13
  374.2 59.4 %copy-start.4 = (bf16[4,128,1024]{2,1,0:T(8,128)(2,1)S(1)}, bf16[4,128,1024]{2,1,0:T(8,128)(2,1)}, u32[]{:S(2)}) copy-start(bf16[4,128,1024]{2,1,0:T(8,128)(2,1)} %all-gather.2.cloned.1.call-done) | copy-start | bytes 3145732
  379.9 55.9 %copy-start.11 = (f32[1024]{0:T(1024)S(1)}, f32[1024]{0:T(1024)}, u32[]{:S(2)}) copy-start(f32[1024]{0:T(1024)} %param.27) | copy-start | bytes 12292
  433.6 2.2 copy-start.1
  433.6 2.5 copy-start.5
  436.1 1.0 copy-start.15
  697.6 316.8 %all-reduce.12.cloned.1.call-start = ((), (), s32[]{:S(2)}) async-start(), calls=%async_computation.4 | async-start | bytes 4194304 | tf_op jit(solution)/shard_map/psum | solution.py:27
  947.7 1.7 copy-start.8
  951.1 65.5 %copy-start.12 = (f32[1024]{0:T(1024)S(1)}, f32[1024]{0:T(1024)}, u32[]{:S(2)}) copy-start(f32[1024]{0:T(1024)} %param.28) | copy-start | bytes 12292
  951.1 140.2 %all-reduce.14.cloned.1.call-start = ((), (), s32[]{:S(2)}) async-start(), calls=%async_computation.5 | async-start | bytes 4194304 | tf_op jit(solution)/shard_map/psum | solution.py:27
  1014.4 2.2 copy-start.2
  1027.6 63.7 %copy-start.6 = (bf16[512,1024]{1,0:T(8,128)(2,1)S(1)}, bf16[512,1024]{1,0:T(8,128)(2,1)}, u32[]{:S(2)}) copy-start(bf16[512,1024]{1,0:T(8,128)(2,1)} %multiply_convert_fusion) | copy-start | bytes 3145732
Sparse Core Ops, SparseCore 0:
  9.1 30.0 all-gather.1
  186.7 180.5 all-reduce.5
  370.8 62.7 all-reduce.7
  697.7 181.0 all-reduce.9
  951.2 63.1 all-reduce.11
  1027.8 63.5 all-reduce.13
where the time goes:
time: 1100 us
  blocking collectives  751 us (68%)
  waiting for transfers between devices  243 us (22%)
  matrix products  40.3 us (4%)
  local copies, waits for them, and re-layouts  37.1 us (3%)
  other arithmetic  15.7 us (1%)
  between operations  13.8 us (1%)
    psum x2, blocking collectives, global_totals(): return lax.psum((denom, numer), 'seq')  376 us
    pmax x2, blocking collectives, global_max(): return lax.pmax(local_max, 'seq')  375 us
    psum x3, waiting for transfers between devices, reduce_norm(): total = lax.psum(partial_value, 'tensor')  176 us
    psum x2, waiting for transfers between devices, global_totals(): return lax.psum((denom, numer), 'seq')  44.2 us
  transfers between devices with their start and end apart: 6, of which 5 were waited for; matrix products, arithmetic and copies ran while one was open for 3% of the time, Pallas kernels for 0%

commit v1 on v0

--- a/solution.py
+++ b/solution.py
@@ -24,7 +24,27 @@
 
 def reduce_norm(residual, partial_value, gain):
     width = residual.shape[1]
-    total = lax.psum(partial_value, "tensor")
+
+    def expand_the_body(buf):
+        link_axis = "tensor"
+        total_devices = lax.axis_size(link_axis)
+
+        def write_terms(spare, x_now):
+            if x_now >= total_devices:
+                return spare
+            last = write_terms(
+                spare
+                + lax.ppermute(
+                    spare, link_axis, list(map(lambda ii: (ii, ii ^ x_now), range(total_devices)))
+                ),
+                2 * x_now,
+            )
+            return last
+
+        z1 = write_terms(buf, 1)
+        return z1
+
+    total = expand_the_body(partial_value)
     full = layer_norm(residual.astype(jnp.float32) + total, gain).astype(jnp.bfloat16)
     columns = width // lax.axis_size("tensor")
     return (full, lax.dynamic_slice_in_dim(full, lax.axis_index("tensor") * columns, columns, 1))

time: 1100 us -> 1200 us (1.091); the launches traced: 1100 us -> 1180 us
  waiting for transfers between devices: 243 us -> 310 us
    ppermute x0 -> x6, waiting for transfers between devices: none -> 244 us  [write_terms(): lax.ppermute(spare, link_axis, list(map(lambda ii: (ii, ii ^ x_now), rang...]
    psum x3 -> x0, waiting for transfers between devices: 176 us -> none  [reduce_norm(): total = lax.psum(partial_value, 'tensor')]
  transfers between devices with their start and end apart: 6 -> 9, of which waited for: 5 -> 8; matrix products, arithmetic and copies ran while one was open for 3% -> 3% of each run, Pallas kernels for 0% -> 0%
where the time goes in v1:
time: 1200 us; the launch traced here: 1180 us
  blocking collectives  755 us (63%)
  waiting for transfers between devices  310 us (26%)
  matrix products  37.3 us (3%)
  local copies, waits for them, and re-layouts  35.7 us (3%)
  other arithmetic  19.5 us (2%)
  between operations  13.5 us (1%)
    pmax x2, blocking collectives, global_max(): return lax.pmax(local_max, 'seq')  380 us
    psum x2, blocking collectives, global_totals(): return lax.psum((denom, numer), 'seq')  376 us
    ppermute x6, waiting for transfers between devices, write_terms(): lax.ppermute(spare, link_axis, list(map(lambda ii: (ii, ii ^ x_now), rang...  244 us
    psum x2, waiting for transfers between devices, global_totals(): return lax.psum((denom, numer), 'seq')  44.1 us
  transfers between devices with their start and end apart: 9, of which 8 were waited for; matrix products, arithmetic and copies ran while one was open for 3% of the time, Pallas kernels for 0%

profile of v1, /device:TPU:1, one launch (start us, length us, event | category | flops | bytes accessed | tf_op | source)
XLA Modules:
  0.0 1179.3 jit_solution(15082837149224939632)
XLA Ops:
  6.5 0.7 all-gather.2.cloned.1.call-update
  7.3 3.9 fusion.135
  11.2 2.6 copy.103
  13.8 2.7 copy.147
  16.5 0.6 fusion.10
  17.3 0.4 compare_reduce_fusion
  17.8 21.5 %all-gather.2.cloned.1.call-done = bf16[4,128,1024]{2,1,0:T(8,128)(2,1)} async-done(((bf16[4,128,256]{2,1,0:T(8,128)(2,1)}), bf16[4,128,1024]{2,1,0:T(8,128)(2,1)}) %all-gather.2.cloned.1.call-update) | async-done | bytes 1048592 | tf_op jit(solution)/shard_map/all_gather | solution.py:73
  39.3 1.7 fusion.12
  41.0 1.0 reshape.249
  42.3 2.0 select_reduce_fusion.2
  44.4 2.2 convolution_convert_fusion.3
  46.6 2.0 reshape.250
  48.7 3.0 fusion.60
  51.6 1.6 copy.110
  53.5 128.2 %pmax.14 = f32[4,128,4]{1,2,0:T(4,128)S(1)} all-reduce(f32[4,128,4]{1,2,0:T(4,128)S(1)} %fusion.97), channel_id=1, replica_groups=mesh['seq'=64,'tensor'=4] {'seq'}, use_global_device_ids=true, to_apply=%region_7.8 | all-reduce | flops 2048 | bytes 16384 | tf_op jit(solution)/shard_map/pmax | solution.py:18
  182.1 0.4 fusion.73
  182.7 2.4 convolution_bitcast_fusion.2
  185.1 1.5 convolution_bitcast_fusion.1
  186.6 1.2 copy.119
  187.8 1.5 convolution_convert_fusion.2
  189.3 1.1 reshape.251
  190.4 1.9 fusion.58
  192.5 1.3 copy.120
  193.8 129.3 %psum.29 = f32[4,128,4]{1,2,0:T(4,128)S(1)} all-reduce(f32[4,128,4]{1,2,0:T(4,128)S(1)} %convolution_bitcast_fusion.4), channel_id=1, replica_groups=mesh['seq'=64,'tensor'=4] {'seq'}, use_global_device_ids=true, to_apply=%region_10.11 | all-reduce | flops 2048 | bytes 16384 | tf_op jit(solution)/shard_map/psum | solution.py:22
  323.1 44.1 %all-reduce.3.cloned.1.call-done = f32[4,128,4,64]{1,3,2,0:T(8,128)} async-done(((f32[4,128,4,64]{1,3,2,0:T(8,128)}), f32[4,128,4,64]{1,3,2,0:T(8,128)}) %all-reduce.3.cloned.1.call-update) | async-done | bytes 524304 | tf_op jit(solution)/shard_map/psum | solution.py:22
  367.3 1.3 fusion.57
  368.8 0.5 fusion.69
  369.2 1.3 collective-permute-start
  370.5 43.1 %collective-permute-done = f32[512,1024]{1,0:T(8,128)S(1)} collective-permute-done((f32[512,1024]{1,0:T(8,128)S(1)}, f32[512,1024]{1,0:T(8,128)S(1)}, u32[]{:S(2)}, u32[]{:S(2)}) %collective-permute-start) | collective-permute-done | bytes 2097184 | tf_op jit(solution)/shard_map/ppermute | solution.py:37
  413.6 1.7 add.131
  415.4 2.7 collective-permute-start.1
  418.0 2.1 fusion.136
  420.1 1.5 copy.148
  421.6 2.5 copy.129
  424.1 0.4 copy.149
  424.5 2.5 copy.131
  427.2 33.4 %collective-permute-done.1 = f32[512,1024]{1,0:T(8,128)} collective-permute-done((f32[512,1024]{1,0:T(8,128)}, f32[512,1024]{1,0:T(8,128)}, u32[]{:S(2)}, u32[]{:S(2)}) %collective-permute-start.1) | collective-permute-done | bytes 2097184 | tf_op jit(solution)/shard_map/ppermute | solution.py:37
  460.6 3.0 fusion.134
  463.6 1.3 copy-done.2
  464.9 0.5 fusion.13
  465.7 1.0 fusion.14
  466.7 2.2 copy.128
  469.0 3.9 select_reduce_fusion
  472.9 251.3 %pmax.15 = f32[4,128,4]{0,2,1:T(4,128)S(1)} all-reduce(f32[4,128,4]{0,2,1:T(4,128)} %get-tuple-element.32), channel_id=1, replica_groups=mesh['seq'=64,'tensor'=4] {'seq'}, use_global_device_ids=true, to_apply=%region_15.16 | all-reduce | flops 2048 | bytes 16384 | tf_op jit(solution)/shard_map/pmax | solution.py:18
  724.2 3.1 fusion.50
  727.3 2.4 copy.132
  729.7 2.4 fusion.48
  732.2 246.2 %psum.31 = f32[4,128,4]{0,2,1:T(4,128)S(1)} all-reduce(f32[4,128,4]{0,2,1:T(4,128)S(1)} %fusion.48), channel_id=1, replica_groups=mesh['seq'=64,'tensor'=4] {'seq'}, use_global_device_ids=true, to_apply=%region_18.19 | all-reduce | flops 2048 | bytes 16384 | tf_op jit(solution)/shard_map/psum | solution.py:22
  978.5 1.4 fusion.15
  980.1 0.5 fusion.66
  980.6 1.3 collective-permute-start.2
  981.9 40.4 %collective-permute-done.2 = f32[512,1024]{1,0:T(8,128)S(1)} collective-permute-done((f32[512,1024]{1,0:T(8,128)S(1)}, f32[512,1024]{1,0:T(8,128)S(1)}, u32[]{:S(2)}, u32[]{:S(2)}) %collective-permute-start.2) | collective-permute-done | bytes 2097184 | tf_op jit(solution)/shard_map/ppermute | solution.py:37
  1022.2 0.4 add.137
  1022.6 3.0 collective-permute-start.3
  1025.6 44.6 %collective-permute-done.3 = f32[512,1024]{1,0:T(8,128)S(1)} collective-permute-done((f32[512,1024]{1,0:T(8,128)S(1)}, f32[512,1024]{1,0:T(8,128)S(1)}, u32[]{:S(2)}, u32[]{:S(2)}) %collective-permute-start.3) | collective-permute-done | bytes 2097184 | tf_op jit(solution)/shard_map/ppermute | solution.py:37
  1070.2 1.9 fusion.133
  1072.2 9.8 fusion.16
  1082.0 41.9 %collective-permute-done.4 = f32[512,1024]{1,0:T(8,128)S(1)} collective-permute-done((f32[512,1024]{1,0:T(8,128)}, f32[512,1024]{1,0:T(8,128)S(1)}, u32[]{:S(2)}, u32[]{:S(2)}) %collective-permute-start.4) | collective-permute-done | bytes 2097184 | tf_op jit(solution)/shard_map/ppermute | solution.py:37
  1123.8 2.0 add.141
  1125.8 1.3 copy-done.4
  1127.1 0.8 dynamic-slice
  1127.9 40.2 %collective-permute-done.5 = f32[512,1024]{1,0:T(8,128)} collective-permute-done((f32[512,1024]{1,0:T(8,128)S(1)}, f32[512,1024]{1,0:T(8,128)}, u32[]{:S(2)}, u32[]{:S(2)}) %collective-permute-start.5) | collective-permute-done | bytes 2097184 | tf_op jit(solution)/shard_map/ppermute | solution.py:37
  1168.1 3.7 fusion.132
  1171.9 0.9 fusion.54
  (68 shorter events, 2.8 us)
Async XLA Ops:
  6.5 1065.6 %copy-start = (bf16[1024,1024]{1,0:T(8,128)(2,1)S(1)}, bf16[1024,1024]{1,0:T(8,128)(2,1)}, u32[]{:S(2)}) copy-start(bf16[1024,1024]{1,0:T(8,128)(2,1)} %param.26) | copy-start | bytes 6291460
  6.5 32.7 %all-gather.2.cloned.1.call-start = ((), (), s32[]{:S(2)}) async-start(), calls=%async_computation | async-start | bytes 1310720 | tf_op jit(solution)/shard_map/all_gather | solution.py:73
  7.3 360.0 %all-reduce.3.cloned.1.call-start = ((), (), s32[]{:S(2)}) async-start(), calls=%async_computation.1 | async-start | bytes 1048576 | tf_op jit(solution)/shard_map/psum | solution.py:22
  13.8 2.7 copy-start.9
  13.8 3.3 copy-start.16
  13.8 3.9 copy-start.10
  13.8 25.5 %copy-start.14 = (bf16[1024,256]{1,0:T(8,128)(2,1)S(1)}, bf16[1024,256]{1,0:T(8,128)(2,1)}, u32[]{:S(2)}) copy-start(bf16[1024,256]{1,0:T(8,128)(2,1)} %param.19) | copy-start | bytes 1572868
  40.9 3.5 copy-start.5
  186.5 792.0 %all-reduce.5.cloned.1.call-start = ((), (), s32[]{:S(2)}) async-start(), calls=%async_computation.2 | async-start | bytes 1048576 | tf_op jit(solution)/shard_map/psum | solution.py:22
  193.8 175.0 %copy-start.7 = (bf16[256,1024]{1,0:T(8,128)(2,1)S(1)}, bf16[256,1024]{1,0:T(8,128)(2,1)}, u32[]{:S(2)}) copy-start(bf16[256,1024]{1,0:T(8,128)(2,1)} %param.22) | copy-start | bytes 1572868
  369.2 44.4 %collective-permute-start = (f32[512,1024]{1,0:T(8,128)S(1)}, f32[512,1024]{1,0:T(8,128)S(1)}, u32[]{:S(2)}, u32[]{:S(2)}) collective-permute-start(f32[512,1024]{1,0:T(8,128)S(1)} %fusion.69), channel_id=1, source_target_pairs={{0,1},{1,0},{2,3},{3,2},{4,5},{5,4},{6,7},{7,6},{8,9},{9,8},{10,11... | collective-permute-start | bytes 6291464 | tf_op jit(solution)/shard_map/ppermute | solution.py:37
  415.4 45.3 %collective-permute-start.1 = (f32[512,1024]{1,0:T(8,128)}, f32[512,1024]{1,0:T(8,128)}, u32[]{:S(2)}, u32[]{:S(2)}) collective-permute-start(f32[512,1024]{1,0:T(8,128)} %add.131), channel_id=1, source_target_pairs={{0,2},{1,3},{2,0},{3,1},{4,6},{5,7},{6,4},{7,5},{8,10},{9,11},{10,... | collective-permute-start | bytes 6291464 | tf_op jit(solution)/shard_map/ppermute | solution.py:37
  421.6 5.5 copy-start.13
  427.2 37.8 %copy-start.11 = (f32[1024]{0:T(1024)S(1)}, f32[1024]{0:T(1024)}, u32[]{:S(2)}) copy-start(f32[1024]{0:T(1024)} %param.27) | copy-start | bytes 12292
  427.2 37.8 %copy-start.15 = (bf16[1024,256]{1,0:T(8,128)(2,1)S(1)}, bf16[1024,256]{1,0:T(8,128)(2,1)}, u32[]{:S(2)}) copy-start(bf16[1024,256]{1,0:T(8,128)(2,1)} %param.23) | copy-start | bytes 1572868
  463.6 1.4 copy-start.2
  466.7 257.5 %copy-start.6 = (bf16[128,8,4,64]{3,1,2,0:T(8,128)(2,1)S(1)}, bf16[128,8,4,64]{3,1,2,0:T(8,128)(2,1)}, u32[]{:S(2)}) copy-start(bf16[128,8,4,64]{3,1,2,0:T(8,128)(2,1)} %copy.131) | copy-start | bytes 1572868
  729.7 250.4 %copy-start.8 = (bf16[256,1024]{1,0:T(8,128)(2,1)S(1)}, bf16[256,1024]{1,0:T(8,128)(2,1)}, u32[]{:S(2)}) copy-start(bf16[256,1024]{1,0:T(8,128)(2,1)} %param.24) | copy-start | bytes 1572868
  980.6 89.7 %copy-start.3 = (f32[512,1024]{1,0:T(8,128)S(1)}, f32[512,1024]{1,0:T(8,128)}, u32[]{:S(2)}) copy-start(f32[512,1024]{1,0:T(8,128)} %copy-done.2) | copy-start | bytes 6291460
  980.6 41.6 %collective-permute-start.2 = (f32[512,1024]{1,0:T(8,128)S(1)}, f32[512,1024]{1,0:T(8,128)S(1)}, u32[]{:S(2)}, u32[]{:S(2)}) collective-permute-start(f32[512,1024]{1,0:T(8,128)S(1)} %fusion.66), channel_id=1, source_target_pairs={{0,1},{1,0},{2,3},{3,2},{4,5},{5,4},{6,7},{7,6},{8,9},{9,8},{10,11... | collective-permute-start | bytes 6291464 | tf_op jit(solution)/shard_map/ppermute | solution.py:37
  1022.6 49.5 %copy-start.12 = (f32[1024]{0:T(1024)S(1)}, f32[1024]{0:T(1024)}, u32[]{:S(2)}) copy-start(f32[1024]{0:T(1024)} %param.28) | copy-start | bytes 12292
  1022.6 47.6 %collective-permute-start.3 = (f32[512,1024]{1,0:T(8,128)S(1)}, f32[512,1024]{1,0:T(8,128)S(1)}, u32[]{:S(2)}, u32[]{:S(2)}) collective-permute-start(f32[512,1024]{1,0:T(8,128)S(1)} %add.137), channel_id=1, source_target_pairs={{0,2},{1,3},{2,0},{3,1},{4,6},{5,7},{6,4},{7,5},{8,10},{9,11},{10,... | collective-permute-start | bytes 6291464 | tf_op jit(solution)/shard_map/ppermute | solution.py:37
  1082.0 41.9 %collective-permute-start.4 = (f32[512,1024]{1,0:T(8,128)}, f32[512,1024]{1,0:T(8,128)S(1)}, u32[]{:S(2)}, u32[]{:S(2)}) collective-permute-start(f32[512,1024]{1,0:T(8,128)} %fusion.16), channel_id=1, source_target_pairs={{0,1},{1,0},{2,3},{3,2},{4,5},{5,4},{6,7},{7,6},{8,9},{9,8},{10,11... | collective-permute-start | bytes 6291464 | tf_op jit(solution)/shard_map/ppermute | solution.py:37
  1125.8 1.3 copy-start.4
  1127.1 41.0 %collective-permute-start.5 = (f32[512,1024]{1,0:T(8,128)S(1)}, f32[512,1024]{1,0:T(8,128)}, u32[]{:S(2)}, u32[]{:S(2)}) collective-permute-start(f32[512,1024]{1,0:T(8,128)S(1)} %add.141), channel_id=1, source_target_pairs={{0,2},{1,3},{2,0},{3,1},{4,6},{5,7},{6,4},{7,5},{8,10},{9,11},{10,... | collective-permute-start | bytes 6291464 | tf_op jit(solution)/shard_map/ppermute | solution.py:37
  1168.1 4.7 copy-start.1
Sparse Core Ops, SparseCore 0:
  9.1 30.0 all-gather.1
  186.7 180.5 all-reduce.2
  729.8 183.1 all-reduce.4
